TPU v7x, 512 devices: a whole 4x4x16 slice. The times are simulated.
512 devices in a mesh: dp: 32 (over y, z_lo, core), ctx: 16 (over x, z_hi).
Axes of the slice: x: 4, y: 4, z: 16 (z_hi: 4, z_lo: 4; z = z_hi * 4 + z_lo), core: 2. Of those that a mesh axis runs over, the one named last changes fastest.
Arguments:
- branch_in: bfloat16 [32, 2048, 2816], P('dp', 'ctx'), may hold values from -6 to 6
- cotangent: bfloat16 [32, 2048, 2816], P('dp', 'ctx'), may hold values from -6 to 6
- weight_a: bfloat16 [256, 2816], P('dp', 'ctx'), may hold values from -0.375 to 0.375
- weight_x: bfloat16 [256, 2816], P('dp', 'ctx'), may hold values from -0.375 to 0.375
- conv_weight: bfloat16 [4, 2816], P(None, 'ctx'), may hold values from -3 to 3
- conv_bias: bfloat16 [2816], P('ctx'), may hold values from -3 to 3
- bias_a: bfloat16 [2816], P('ctx'), may hold values from -4 to 4
- bias_x: bfloat16 [2816], P('ctx'), may hold values from -4 to 4
- rate: bfloat16 [2816], P('ctx'), may hold values from 0 to 0.016, as said below
Outputs:
- grad_input: bfloat16 [32, 2048, 2816], P('dp', 'ctx')
- grad_weight_a: float32 [256, 2816], P('dp', 'ctx')
- grad_rate: float32 [2816], replicated
Inputs may be any that keep to these rules, and one draw needn't show every extreme that they name: `rate`: positive in every channel.
All inputs are finite; a program needn't handle non-finite values.
Results may differ from a plain program's by a relative error of at most 0.006.
Values may be sent and summed in bfloat16 or wider, within the bound.
No kernel may reach another device: no remote copies, remote signals or barrier semaphores. Data moves between devices by JAX's collectives and lax.ppermute only.
A program may use at most 128 MiB of HBM per device.

v0:
```python
import math
import jax
import jax.numpy as jnp
from jax import lax
from jax.sharding import PartitionSpec as P

floor_value = 2.5e-07


def passed_along(array, axis, by):
    length = lax.axis_size(axis)
    pairs = [(i, i + by) for i in range(length) if 0 <= i + by < length]
    return lax.ppermute(array, axis, pairs)


def mix_heads(values, weights):
    tokens = values.shape[0]
    head_width = weights.shape[0]
    head_count = weights.shape[1] // head_width
    left = values.reshape(tokens, head_count, head_width)
    right = weights.reshape(head_width, head_count, head_width)
    result = jnp.einsum("thk,khj->thj", left, right, preferred_element_type=jnp.float32)
    return result.reshape(tokens, head_count * head_width)


def back_heads(grads, weights):
    tokens = grads.shape[0]
    head_width = weights.shape[0]
    head_count = weights.shape[1] // head_width
    left = grads.reshape(tokens, head_count, head_width)
    right = weights.reshape(head_width, head_count, head_width)
    result = jnp.einsum("thj,khj->thk", left, right, preferred_element_type=jnp.float32)
    return result.reshape(tokens, head_count * head_width)


def grad_heads(values, grads, head_width):
    tokens = values.shape[0]
    head_count = values.shape[1] // head_width
    left = values.reshape(tokens, head_count, head_width)
    right = grads.reshape(tokens, head_count, head_width)
    result = jnp.einsum("thk,thj->khj", left, right, preferred_element_type=jnp.float32)
    return result.reshape(head_width, head_count * head_width)


def combine(earlier, later):
    return (earlier[0] * later[0], later[0] * earlier[1] + later[1])


def block_scan(coef, value, reverse):
    length = coef.shape[0]
    width = coef.shape[1]
    block_size = math.gcd(length, 16)
    block_count = length // block_size
    coef_blocks = coef.reshape(block_count, block_size, width)
    value_blocks = value.reshape(block_count, block_size, width)
    visit_order = list(range(block_size))
    if reverse:
        visit_order = visit_order[::-1]
    coef_rows = [None] * block_size
    value_rows = [None] * block_size
    running_coef = None
    running_value = None
    for position in visit_order:
        step_coef = coef_blocks[:, position]
        step_value = value_blocks[:, position]
        if running_coef is None:
            running_coef = step_coef
            running_value = step_value
        else:
            running_value = step_coef * running_value + step_value
            running_coef = running_coef * step_coef
        coef_rows[position] = running_coef
        value_rows[position] = running_value
    local_coef = jnp.stack(coef_rows, 1)
    local_value = jnp.stack(value_rows, 1)
    edge = 0 if reverse else block_size - 1
    summary_coef = local_coef[:, edge]
    summary_value = local_value[:, edge]
    incl_coef, incl_value = lax.associative_scan(
        combine, (summary_coef, summary_value), reverse=reverse, axis=0
    )
    ones_row = jnp.ones((1, width), jnp.float32)
    zero_row = jnp.zeros((1, width), jnp.float32)
    if reverse:
        prior_coef = jnp.concatenate([incl_coef[1:], ones_row], 0)
        prior_value = jnp.concatenate([incl_value[1:], zero_row], 0)
    else:
        prior_coef = jnp.concatenate([ones_row, incl_coef[:-1]], 0)
        prior_value = jnp.concatenate([zero_row, incl_value[:-1]], 0)
    whole_coef = local_coef * prior_coef[:, None]
    whole_value = local_coef * prior_value[:, None] + local_value
    return (whole_coef.reshape(length, width), whole_value.reshape(length, width))


def on_device(
    branch_in, cotangent, weight_a, weight_x, conv_weight, conv_bias, bias_a, bias_x, rate
):
    inputs = branch_in[0]
    upstream = cotangent[0].astype(jnp.float32)
    length = inputs.shape[0]
    taps = conv_weight.shape[0]
    packed = jnp.concatenate(
        [conv_weight, conv_bias[None], bias_a[None], bias_x[None], rate[None]], 0
    )
    rows_a, rows_x = (
        lax.all_gather(weight_a, "dp", axis=0, tiled=True),
        lax.all_gather(weight_x, "dp", axis=0, tiled=True),
    )
    full_a, full_x, params = (
        lax.all_gather(rows_a, "ctx", axis=1, tiled=True),
        lax.all_gather(rows_x, "ctx", axis=1, tiled=True),
        lax.all_gather(packed, "ctx", axis=1, tiled=True),
    )
    params = params.astype(jnp.float32)
    taps_f = params[:taps]
    cbias = params[taps]
    abias = params[taps + 1]
    xbias = params[taps + 2]
    rates = params[taps + 3]
    width = params.shape[1]
    head_width = full_a.shape[0]
    tail = passed_along(inputs[length - (taps - 1) :], "ctx", 1)
    padded = jnp.concatenate([tail, inputs], 0).astype(jnp.float32)
    conv = cbias
    for tap in range(taps):
        conv = conv + taps_f[tap] * padded[tap : tap + length]
    conv_b = conv.astype(jnp.bfloat16)
    conv_f = conv_b.astype(jnp.float32)
    recur_gate = jax.nn.sigmoid(mix_heads(conv_b, full_a) + abias)
    input_gate = jax.nn.sigmoid(mix_heads(conv_b, full_x) + xbias)
    log_decay = -8.0 * recur_gate * rates
    decay = jnp.exp(log_decay)
    one_minus = -jnp.expm1(2.0 * log_decay)
    multiplier = jnp.sqrt(jnp.maximum(one_minus, floor_value))
    drive = multiplier * input_gate * conv_f
    cum_decay, local_hidden = block_scan(decay, drive, False)
    zero_row = jnp.zeros((width,), jnp.float32)
    span = lax.axis_size("ctx")

    def forward_turn(turn, incoming):
        outgoing = cum_decay[-1] * incoming + local_hidden[-1]
        return passed_along(outgoing, "ctx", 1)

    state_in = lax.fori_loop(0, span - 1, forward_turn, zero_row)
    hidden = local_hidden + cum_decay * state_in
    previous = jnp.concatenate([state_in[None], hidden[:-1]], 0)
    coefs = jnp.concatenate([decay[1:], jnp.ones((1, width), jnp.float32)], 0)
    cum_coef, local_back = block_scan(coefs, upstream, True)
    head_coef = decay[0] * cum_coef[0]
    head_value = decay[0] * local_back[0]

    def backward_turn(turn, incoming):
        outgoing = head_coef * incoming + head_value
        return passed_along(outgoing, "ctx", -1)

    back_in = lax.fori_loop(0, span - 1, backward_turn, zero_row)
    back = local_back + cum_coef * back_in
    slope = jnp.where(one_minus > floor_value, 0.5 / multiplier, 0.0)
    d_mult = back * input_gate * conv_f
    d_log = back * previous * decay - 2.0 * decay * decay * d_mult * slope
    d_recur = (d_log * (-8.0 * rates) * recur_gate * (1.0 - recur_gate)).astype(jnp.bfloat16)
    d_input = (back * multiplier * conv_f * input_gate * (1.0 - input_gate)).astype(jnp.bfloat16)
    d_conv = (
        back * multiplier * input_gate + back_heads(d_recur, full_a) + back_heads(d_input, full_x)
    )
    following = passed_along(d_conv[: taps - 1], "ctx", -1)
    dpad = jnp.concatenate([d_conv, following], 0)
    grad_in = jnp.zeros((length, width), jnp.float32)
    for tap in range(taps):
        start = taps - 1 - tap
        grad_in = grad_in + taps_f[tap] * dpad[start : start + length]
    local_wgrad = grad_heads(conv_b, d_recur, head_width)
    row_part = lax.psum_scatter(local_wgrad, "dp", scatter_dimension=0, tiled=True)
    wgrad = lax.psum_scatter(row_part, "ctx", scatter_dimension=1, tiled=True)
    rgrad = lax.psum(jnp.sum(d_log * (-8.0 * recur_gate), axis=0), ("dp", "ctx"))
    return (grad_in.astype(jnp.bfloat16)[None], wgrad, rgrad)


def solution(mesh):
    placed = (
        P("dp", "ctx", None),
        P("dp", "ctx", None),
        P("dp", "ctx"),
        P("dp", "ctx"),
        P(None, "ctx"),
        P("ctx"),
        P("ctx"),
        P("ctx"),
        P("ctx"),
    )
    return jax.shard_map(
        on_device,
        mesh=mesh,
        in_specs=placed,
        out_specs=(P("dp", "ctx", None), P("dp", "ctx"), P()),
        check_vma=False,
    )
```

profile of v0, /device:TPU:8, one launch (start us, length us, event | category | flops | bytes accessed | tf_op | source)
XLA Modules:
  0.0 1052.8 jit_solution(17856726429922451769)
XLA Ops:
  7.2 38.4 %all_gather.16 = bf16[256,176]{1,0:T(8,128)(2,1)S(1)} all-gather(bf16[8,176]{1,0:T(8,128)(2,1)} %param.15), channel_id=1, replica_groups=mesh['dp'=32,'ctx'=16] {'dp'}, dimensions={0}, use_global_device_ids=true | all-gather | bytes 92928 | tf_op jit(solution)/shard_map/all_gather | solution.py:106
  47.2 9.1 collective-permute-start.2
  56.3 38.7 %all_gather.18 = bf16[256,176]{1,0:T(8,128)(2,1)S(1)} all-gather(bf16[8,176]{1,0:T(8,128)(2,1)} %param.16), channel_id=1, replica_groups=mesh['dp'=32,'ctx'=16] {'dp'}, dimensions={0}, use_global_device_ids=true | all-gather | bytes 92928 | tf_op jit(solution)/shard_map/all_gather | solution.py:107
  99.2 55.8 %all-gather = bf16[16,176,8]{1,2,0:T(8,128)(2,1)S(1)} all-gather(bf16[1,176,8]{1,2,0:T(8,128)(2,1)S(1)} %bitcast.278), channel_id=1, replica_groups=mesh['dp'=32,'ctx'=16] {'ctx'}, dimensions={0}, use_global_device_ids=true | all-gather | bytes 47872 | tf_op jit(solution)/shard_map/all_gather | solution.py:112
  185.2 35.6 %all-gather.6.cloned.1.call-done = bf16[256,2816]{0,1:T(8,128)(2,1)} async-done(((bf16[256,176]{0,1:T(8,128)(2,1)}), bf16[256,2816]{0,1:T(8,128)(2,1)}) %all-gather.6.cloned.1.call-update) | async-done | bytes 1441808 | tf_op jit(solution)/shard_map/all_gather | solution.py:111
  270.9 10.1 slice.532
  281.0 10.1 slice.525
  291.0 10.1 slice.529
  301.1 10.1 slice.527
  392.6 166.2 %while.21 = (s32[]{:T(128)}, f32[2816]{0:T(1024)S(1)}, f32[128,2816]{1,0:T(8,128)}, f32[128,2816]{1,0:T(8,128)}, s32[]{:T(128)}) while((s32[]{:T(128)}, f32[2816]{0:T(1024)S(1)}, f32[128,2816]{1,0:T(8,128)}, f32[128,2816]{1,0:T(8,128)}, s32[]{:T(128)}) %tuple.181), condition=%wide.region_3.0_spmd, body=%wide.region_2.0_spmd.sunk | while | flops 5634 | bytes 135269 | solution.py:144
  595.8 158.0 %while.20 = (s32[]{:T(128)}, f32[2816]{0:T(1024)S(1)}, f32[2816]{0:T(1024)S(1)}, f32[2816]{0:T(1024)S(1)}, s32[]{:T(128)}) while((s32[]{:T(128)}, f32[2816]{0:T(1024)S(1)}, f32[2816]{0:T(1024)S(1)}, f32[2816]{0:T(1024)S(1)}, s32[]{:T(128)}) %tuple.169), condition=%wide.region_1.0_spmd, body=%wide.region_0.0_spmd.sunk | while | flops 5634 | bytes 90213 | solution.py:156
  597.1 9.4 collective-permute-done
  607.8 9.4 collective-permute-done
  618.5 9.8 collective-permute-done
  629.5 9.4 collective-permute-done
  640.2 9.2 collective-permute-done
  650.7 9.1 collective-permute-done
  671.4 9.5 collective-permute-done
  692.2 9.3 collective-permute-done
  702.8 9.5 collective-permute-done
  734.3 9.1 collective-permute-done
  782.9 114.6 %psum.7 = f32[2816]{0:T(1024)} all-reduce(f32[2816]{0:T(1024)S(1)} %get-tuple-element.94), channel_id=1, replica_groups=mesh['dp'=32,'ctx'=16] {'dp','ctx'}, use_global_device_ids=true, to_apply=%region_7.8 | all-reduce | flops 2816 | bytes 22528 | tf_op jit(solution)/shard_map/psum | solution.py:175
  898.0 9.7 reduce-scatter.5.cloned.1.call-done
  917.2 127.5 %reduce-scatter.7.cloned.1.call-done = f32[176,8]{1,0:T(8,128)} async-done(((f32[2816,8]{1,0:T(8,128)}), f32[176,8]{1,0:T(8,128)}) %reduce-scatter.7.cloned.1.call-update) | async-done | bytes 5648
  (492 shorter events, 474.0 us)
Async XLA Ops:
  7.2 159.0 %all-gather.4.cloned.1.call-start = ((), (), s32[]{:S(2)}) async-start(), calls=%async_computation.2 | async-start | bytes 1531904 | tf_op jit(solution)/shard_map/all_gather | solution.py:110
  46.4 174.4 %all-gather.6.cloned.1.call-start = ((), (), s32[]{:S(2)}) async-start(), calls=%async_computation.3 | async-start | bytes 1531904 | tf_op jit(solution)/shard_map/all_gather | solution.py:111
  47.2 111.4 %collective-permute-start.2 = (bf16[3,2816]{1,0:T(4,128)(2,1)S(1)}, bf16[3,2816]{1,0:T(4,128)(2,1)S(1)}, u32[]{:S(2)}, u32[]{:S(2)}) collective-permute-start(bf16[3,2816]{1,0:T(4,128)(2,1)S(1)} %slice_bitcast_fusion), channel_id=1, source_target_pairs={{0,1},{1,2},{2,3},{3,4},{4,5},{5,6},{6,7},{7,8},{8,9},{9,10},{10,1... | collective-permute-start | bytes 50696 | tf_op jit(solution)/shard_map/ppermute | solution.py:13
  95.8 811.9 %reduce-scatter.5.cloned.1.call-start = ((), (), s32[]{:S(2)}) async-start(), calls=%async_computation.4 | async-start | bytes 2973696 | tf_op jit(solution)/shard_map/reduce_scatter | solution.py:173
  434.0 9.8 collective-permute-start.1
  536.0 10.6 %collective-permute-start.1 = (f32[2816]{0:T(1024)}, f32[2816]{0:T(1024)S(1)}, u32[]{:S(2)}, u32[]{:S(2)}) collective-permute-start(f32[2816]{0:T(1024)} %multiply_add_fusion.31), channel_id=1, source_target_pairs={{0,1},{1,2},{2,3},{3,4},{4,5},{5,6},{6,7},{7,8},{8,9},{9,10},{10,1... | collective-permute-start | bytes 33800 | tf_op jit(solution)/shard_map/while/body/eval_jaxpr/ppermute | solution.py:13
  548.2 10.6 %collective-permute-start.1 = (f32[2816]{0:T(1024)}, f32[2816]{0:T(1024)S(1)}, u32[]{:S(2)}, u32[]{:S(2)}) collective-permute-start(f32[2816]{0:T(1024)} %multiply_add_fusion.31), channel_id=1, source_target_pairs={{0,1},{1,2},{2,3},{3,4},{4,5},{5,6},{6,7},{7,8},{8,9},{9,10},{10,1... | collective-permute-start | bytes 33800 | tf_op jit(solution)/shard_map/while/body/eval_jaxpr/ppermute | solution.py:13
  595.8 10.7 %collective-permute-start = (f32[2816]{0:T(1024)S(1)}, f32[2816]{0:T(1024)S(1)}, u32[]{:S(2)}, u32[]{:S(2)}) collective-permute-start(f32[2816]{0:T(1024)S(1)} %multiply_add_fusion.30), channel_id=1, source_target_pairs={{1,0},{2,1},{3,2},{4,3},{5,4},{6,5},{7,6},{8,7},{9,8},{10,9},{11,1... | collective-permute-start | bytes 33800 | tf_op jit(solution)/shard_map/while/body/eval_jaxpr/ppermute | solution.py:13
  606.5 10.7 %collective-permute-start = (f32[2816]{0:T(1024)S(1)}, f32[2816]{0:T(1024)S(1)}, u32[]{:S(2)}, u32[]{:S(2)}) collective-permute-start(f32[2816]{0:T(1024)S(1)} %multiply_add_fusion.30), channel_id=1, source_target_pairs={{1,0},{2,1},{3,2},{4,3},{5,4},{6,5},{7,6},{8,7},{9,8},{10,9},{11,1... | collective-permute-start | bytes 33800 | tf_op jit(solution)/shard_map/while/body/eval_jaxpr/ppermute | solution.py:13
  617.2 11.1 %collective-permute-start = (f32[2816]{0:T(1024)S(1)}, f32[2816]{0:T(1024)S(1)}, u32[]{:S(2)}, u32[]{:S(2)}) collective-permute-start(f32[2816]{0:T(1024)S(1)} %multiply_add_fusion.30), channel_id=1, source_target_pairs={{1,0},{2,1},{3,2},{4,3},{5,4},{6,5},{7,6},{8,7},{9,8},{10,9},{11,1... | collective-permute-start | bytes 33800 | tf_op jit(solution)/shard_map/while/body/eval_jaxpr/ppermute | solution.py:13
  628.3 10.7 %collective-permute-start = (f32[2816]{0:T(1024)S(1)}, f32[2816]{0:T(1024)S(1)}, u32[]{:S(2)}, u32[]{:S(2)}) collective-permute-start(f32[2816]{0:T(1024)S(1)} %multiply_add_fusion.30), channel_id=1, source_target_pairs={{1,0},{2,1},{3,2},{4,3},{5,4},{6,5},{7,6},{8,7},{9,8},{10,9},{11,1... | collective-permute-start | bytes 33800 | tf_op jit(solution)/shard_map/while/body/eval_jaxpr/ppermute | solution.py:13
  638.9 10.5 collective-permute-start
  649.4 10.4 collective-permute-start
  659.8 10.3 collective-permute-start
  670.1 10.7 %collective-permute-start = (f32[2816]{0:T(1024)S(1)}, f32[2816]{0:T(1024)S(1)}, u32[]{:S(2)}, u32[]{:S(2)}) collective-permute-start(f32[2816]{0:T(1024)S(1)} %multiply_add_fusion.30), channel_id=1, source_target_pairs={{1,0},{2,1},{3,2},{4,3},{5,4},{6,5},{7,6},{8,7},{9,8},{10,9},{11,1... | collective-permute-start | bytes 33800 | tf_op jit(solution)/shard_map/while/body/eval_jaxpr/ppermute | solution.py:13
  680.9 10.0 collective-permute-start
  690.9 10.6 %collective-permute-start = (f32[2816]{0:T(1024)S(1)}, f32[2816]{0:T(1024)S(1)}, u32[]{:S(2)}, u32[]{:S(2)}) collective-permute-start(f32[2816]{0:T(1024)S(1)} %multiply_add_fusion.30), channel_id=1, source_target_pairs={{1,0},{2,1},{3,2},{4,3},{5,4},{6,5},{7,6},{8,7},{9,8},{10,9},{11,1... | collective-permute-start | bytes 33800 | tf_op jit(solution)/shard_map/while/body/eval_jaxpr/ppermute | solution.py:13
  701.5 10.8 %collective-permute-start = (f32[2816]{0:T(1024)S(1)}, f32[2816]{0:T(1024)S(1)}, u32[]{:S(2)}, u32[]{:S(2)}) collective-permute-start(f32[2816]{0:T(1024)S(1)} %multiply_add_fusion.30), channel_id=1, source_target_pairs={{1,0},{2,1},{3,2},{4,3},{5,4},{6,5},{7,6},{8,7},{9,8},{10,9},{11,1... | collective-permute-start | bytes 33800 | tf_op jit(solution)/shard_map/while/body/eval_jaxpr/ppermute | solution.py:13
  712.4 10.3 collective-permute-start
  722.6 10.4 collective-permute-start
  733.0 10.4 collective-permute-start
  743.4 10.4 collective-permute-start
  767.5 277.2 %reduce-scatter.7.cloned.1.call-start = ((), (), s32[]{:S(2)}) async-start(), calls=%async_computation.5 | async-start | bytes 1531904
  781.6 115.9 %collective-permute-start.3 = (f32[3,2816]{1,0:T(4,128)S(1)}, f32[3,2816]{1,0:T(4,128)S(1)}, u32[]{:S(2)}, u32[]{:S(2)}) collective-permute-start(f32[3,2816]{1,0:T(4,128)S(1)} %copy.775), channel_id=1, source_target_pairs={{1,0},{2,1},{3,2},{4,3},{5,4},{6,5},{7,6},{8,7},{9,8},{10,9},{11,1... | collective-permute-start | bytes 101384 | tf_op jit(solution)/shard_map/ppermute | solution.py:13
  (109 other events, 1956.0 us)
Sparse Core Ops, SparseCore 0:
  46.5 93.5 all-gather.3
  143.1 77.5 all-gather.5
  767.7 139.9 reduce-scatter.4
  911.6 133.0 reduce-scatter.6
where the time goes:
time: 1060 us; the launch traced here: 1050 us
  waiting for transfers between devices  335 us (32%)
  blocking collectives  248 us (23%)
  local copies, waits for them, and re-layouts  192 us (18%)
  starting transfers between devices  148 us (14%)
  other arithmetic  104 us (10%)
  between operations  15 us (1%)
    ppermute x32, waiting for transfers between devices, passed_along(): return lax.ppermute(array, axis, pairs)  162 us
    ppermute x32, starting transfers between devices, passed_along(): return lax.ppermute(array, axis, pairs)  148 us
    unnamed x5, waiting for transfers between devices  128 us
    psum x1, blocking collectives, on_device(): lax.psum(jnp.sum(d_log * (-8.0 * recur_gate), axis=0), ('dp', 'ctx'))  115 us
    slice x30, local copies, waits for them, and re-layouts, block_scan(): lax.associative_scan(combine, (summary_coef, summary_value), reverse=reve...  62.1 us
    all_gather x1, blocking collectives, on_device(): lax.all_gather(packed, 'ctx', axis=1, tiled=True)  55.8 us
    all_gather x1, blocking collectives, on_device(): lax.all_gather(weight_x, 'dp', axis=0, tiled=True)  38.7 us
    all_gather x1, blocking collectives, on_device(): lax.all_gather(weight_a, 'dp', axis=0, tiled=True)  38.4 us
  transfers between devices with their start and end apart: 36, of which 33 were waited for; matrix products, arithmetic and copies ran while one was open for 5% of the time, Pallas kernels for 0%

commit v1 on v0

--- a/solution.py
+++ b/solution.py
@@ -172,7 +172,9 @@
     local_wgrad = grad_heads(conv_b, d_recur, head_width)
     row_part = lax.psum_scatter(local_wgrad, "dp", scatter_dimension=0, tiled=True)
     wgrad = lax.psum_scatter(row_part, "ctx", scatter_dimension=1, tiled=True)
-    rgrad = lax.psum(jnp.sum(d_log * (-8.0 * recur_gate), axis=0), ("dp", "ctx"))
+    q_in = jnp.sum(d_log * (-8.0 * recur_gate), axis=0)
+    seen_now = jax.lax.all_gather(q_in, ("dp", "ctx"))
+    rgrad = jnp.sum(seen_now, axis=0)
     return (grad_in.astype(jnp.bfloat16)[None], wgrad, rgrad)
 
 

time: 1060 us -> 2470 us (2.33)
  the two profiles are of different devices: /device:TPU:8 before, /device:TPU:99 now
where the time goes in v1:
time: 2470 us; the launch traced here: 2460 us
  waiting for transfers between devices  1860 us (75%)
  local copies, waits for them, and re-layouts  190 us (8%)
  starting transfers between devices  146 us (6%)
  blocking collectives  124 us (5%)
  other arithmetic  111 us (4%)
    all_gather x1, waiting for transfers between devices, on_device(): seen_now = jax.lax.all_gather(q_in, ('dp', 'ctx'))  1410 us
    reduce_scatter x1, waiting for transfers between devices, on_device(): lax.psum_scatter(local_wgrad, 'dp', scatter_dimension=0, tiled=True)  168 us
    ppermute x32, waiting for transfers between devices, passed_along(): return lax.ppermute(array, axis, pairs)  146 us
    ppermute x32, starting transfers between devices, passed_along(): return lax.ppermute(array, axis, pairs)  146 us
    unnamed x6, waiting for transfers between devices  102 us
    slice x30, local copies, waits for them, and re-layouts, block_scan(): lax.associative_scan(combine, (summary_coef, summary_value), reverse=reve...  61.4 us
  transfers between devices with their start and end apart: 37, of which 35 were waited for; matrix products, arithmetic and copies ran while one was open for 2% of the time, Pallas kernels for 0%

profile of v1, /device:TPU:99, one launch (start us, length us, event | category | flops | bytes accessed | tf_op | source)
XLA Modules:
  0.0 2459.6 jit_solution(16614530690555824027)
XLA Ops:
  7.2 34.5 %all_gather.22 = bf16[256,176]{1,0:T(8,128)(2,1)S(1)} all-gather(bf16[8,176]{1,0:T(8,128)(2,1)} %param.15), channel_id=1, replica_groups=mesh['dp'=32,'ctx'=16] {'dp'}, dimensions={0}, use_global_device_ids=true | all-gather | bytes 92928 | tf_op jit(solution)/shard_map/all_gather | solution.py:106
  43.3 8.8 collective-permute-start.2
  52.1 44.5 %all_gather.24 = bf16[256,176]{1,0:T(8,128)(2,1)S(1)} all-gather(bf16[8,176]{1,0:T(8,128)(2,1)} %param.16), channel_id=1, replica_groups=mesh['dp'=32,'ctx'=16] {'dp'}, dimensions={0}, use_global_device_ids=true | all-gather | bytes 92928 | tf_op jit(solution)/shard_map/all_gather | solution.py:107
  100.8 45.1 %all-gather.1 = bf16[16,176,8]{1,2,0:T(8,128)(2,1)S(1)} all-gather(bf16[1,176,8]{1,2,0:T(8,128)(2,1)S(1)} %bitcast.278), channel_id=1, replica_groups=mesh['dp'=32,'ctx'=16] {'ctx'}, dimensions={0}, use_global_device_ids=true | all-gather | bytes 47872 | tf_op jit(solution)/shard_map/all_gather | solution.py:112
  176.0 39.2 %all-gather.9.cloned.1.call-done = bf16[256,2816]{0,1:T(8,128)(2,1)} async-done(((bf16[256,176]{0,1:T(8,128)(2,1)}), bf16[256,2816]{0,1:T(8,128)(2,1)}) %all-gather.9.cloned.1.call-update) | async-done | bytes 1441808 | tf_op jit(solution)/shard_map/all_gather | solution.py:111
  264.3 9.9 slice.532
  274.2 10.0 slice.525
  284.2 10.0 slice.529
  294.1 10.0 slice.527
  385.6 165.9 %while.21 = (s32[]{:T(128)}, f32[2816]{0:T(1024)S(1)}, f32[128,2816]{1,0:T(8,128)}, f32[128,2816]{1,0:T(8,128)}, s32[]{:T(128)}) while((s32[]{:T(128)}, f32[2816]{0:T(1024)S(1)}, f32[128,2816]{1,0:T(8,128)}, f32[128,2816]{1,0:T(8,128)}, s32[]{:T(128)}) %tuple.183), condition=%wide.region_3.0_spmd, body=%wide.region_2.0_spmd.sunk | while | flops 5634 | bytes 135269 | solution.py:144
  588.7 132.1 %while.20 = (s32[]{:T(128)}, f32[2816]{0:T(1024)S(1)}, f32[2816]{0:T(1024)S(1)}, f32[2816]{0:T(1024)S(1)}, s32[]{:T(128)}) while((s32[]{:T(128)}, f32[2816]{0:T(1024)S(1)}, f32[2816]{0:T(1024)S(1)}, f32[2816]{0:T(1024)S(1)}, s32[]{:T(128)}) %tuple.169), condition=%wide.region_1.0_spmd, body=%wide.region_0.0_spmd.sunk | while | flops 5634 | bytes 90213 | solution.py:156
  647.1 8.2 collective-permute-start
  656.1 8.4 collective-permute-start
  665.4 8.4 collective-permute-start
  674.6 8.4 collective-permute-start
  683.9 8.4 collective-permute-start
  693.1 8.4 collective-permute-start
  702.3 8.4 collective-permute-start
  711.6 8.4 collective-permute-start
  720.9 8.9 multiply_reduce_fusion
  734.6 167.7 %reduce-scatter.5.cloned.1.call-done = f32[8,2816]{1,0:T(8,128)} async-done(((f32[256,2816]{1,0:T(8,128)}), f32[8,2816]{1,0:T(8,128)}) %reduce-scatter.5.cloned.1.call-update) | async-done | bytes 90128 | tf_op jit(solution)/shard_map/reduce_scatter | solution.py:173
  918.3 8.2 collective-permute-start.3
  935.2 102.2 %reduce-scatter.7.cloned.1.call-done = f32[176,8]{1,0:T(8,128)} async-done(((f32[2816,8]{1,0:T(8,128)}), f32[176,8]{1,0:T(8,128)}) %reduce-scatter.7.cloned.1.call-update) | async-done | bytes 5648
  1038.9 1407.8 %all-gather.11.cloned.1.call-done = f32[512,1,2816]{2,1,0:T(1,128)} async-done(((f32[1,1,2816]{2,1,0:T(1,128)}), f32[512,1,2816]{2,1,0:T(1,128)}) %all-gather.11.cloned.1.call-update) | async-done | bytes 5767184 | tf_op jit(solution)/shard_map/all_gather | solution.py:176
  (496 shorter events, 470.3 us)
Async XLA Ops:
  7.2 149.8 %all-gather.7.cloned.1.call-start = ((), (), s32[]{:S(2)}) async-start(), calls=%async_computation.2 | async-start | bytes 1531904 | tf_op jit(solution)/shard_map/all_gather | solution.py:110
  42.5 172.8 %all-gather.9.cloned.1.call-start = ((), (), s32[]{:S(2)}) async-start(), calls=%async_computation.3 | async-start | bytes 1531904 | tf_op jit(solution)/shard_map/all_gather | solution.py:111
  43.3 106.1 %collective-permute-start.2 = (bf16[3,2816]{1,0:T(4,128)(2,1)S(1)}, bf16[3,2816]{1,0:T(4,128)(2,1)S(1)}, u32[]{:S(2)}, u32[]{:S(2)}) collective-permute-start(bf16[3,2816]{1,0:T(4,128)(2,1)S(1)} %slice_bitcast_fusion), channel_id=1, source_target_pairs={{0,1},{1,2},{2,3},{3,4},{4,5},{5,6},{6,7},{7,8},{8,9},{9,10},{10,1... | collective-permute-start | bytes 50696 | tf_op jit(solution)/shard_map/ppermute | solution.py:13
  97.4 804.9 %reduce-scatter.5.cloned.1.call-start = ((), (), s32[]{:S(2)}) async-start(), calls=%async_computation.4 | async-start | bytes 2973696 | tf_op jit(solution)/shard_map/reduce_scatter | solution.py:173
  387.2 9.4 collective-permute-start.1
  398.2 9.4 collective-permute-start.1
  409.3 9.4 collective-permute-start.1
  420.3 9.4 collective-permute-start.1
  431.4 9.4 collective-permute-start.1
  442.4 9.4 collective-permute-start.1
  453.5 9.5 collective-permute-start.1
  464.6 9.5 collective-permute-start.1
  475.7 9.4 collective-permute-start.1
  486.7 9.4 collective-permute-start.1
  497.8 9.4 collective-permute-start.1
  508.8 9.4 collective-permute-start.1
  519.9 9.5 collective-permute-start.1
  531.0 9.4 collective-permute-start.1
  542.0 9.4 collective-permute-start.1
  674.6 9.2 collective-permute-start
  683.9 9.2 collective-permute-start
  734.6 302.8 %reduce-scatter.7.cloned.1.call-start = ((), (), s32[]{:S(2)}) async-start(), calls=%async_computation.6 | async-start | bytes 1531904
  904.9 1541.9 %all-gather.11.cloned.1.call-start = ((), (), s32[]{:S(2)}) async-start(), calls=%async_computation.5 | async-start | bytes 5778432 | tf_op jit(solution)/shard_map/all_gather | solution.py:176
  918.3 9.3 collective-permute-start.3
  (110 other events, 2156.2 us)
Sparse Core Ops, SparseCore 0:
  42.6 92.0 all-gather.6
  137.8 77.4 all-gather.8
  734.7 167.6 reduce-scatter.4
  906.3 131.0 reduce-scatter.6
  1040.0 1406.6 all-gather.10
